TPU v7x, 128 devices: a whole 4x4x4 slice. The times are simulated.
128 devices in a mesh: band: 4 (over x), pair: 32 (over z, y, core).
Axes of the slice: x: 4, y: 4, z: 4, core: 2. Of those that a mesh axis runs over, the one named last changes fastest.
Arguments:
- traces: float32 [16, 8192, 1024], P('band', 'pair'), may hold values from -300 to 300
- pair_list: int32 [256, 2], replicated, may hold values from 0 to 63, as said below
- pair_owner: int32 [256], replicated, may hold values from 0 to 63, as said below
Outputs:
- cross_spectra: bfloat16 [64, 2, 128, 128, 512], P('pair', None, None, None, 'band')
Inputs may be any that keep to these rules, and one draw needn't show every extreme that they name: `pair_list`: each row (i, j) has 8 <= j - i <= 24; index p of pair holds blocks p * 64 / 32 up to (p + 1) * 64 / 32 - 1, and the 16 blocks named by the rows of one owner (pair_owner // 2) all lie on different indices of pair. `pair_owner`: every slot is named by exactly 4 rows.
All inputs are finite; a program needn't handle non-finite values.
Results may differ from a plain program's by a relative error of at most 0.0057.
Values may be sent and summed in bfloat16 or wider, within the bound.
No kernel may reach another device: no remote copies, remote signals or barrier semaphores. Data moves between devices by JAX's collectives and lax.ppermute only.
A program may use at most 320 MiB of HBM per device.

v0:
```python
import numpy as np
import jax
import jax.numpy as jnp
from jax import lax
from jax.sharding import PartitionSpec as P

SUB = 64
BLOCK = 128
SLOTS = 2
whiten_eps = 1e-05


def dft_table(samples, bins):
    phase_angle = np.arange(samples)[None, :] * bins[:, None] % samples * (2.0 * np.pi / samples)
    return jnp.asarray(
        np.concatenate([np.cos(phase_angle), -np.sin(phase_angle)], axis=0).astype(np.float32)
    )


def whiten(flat_traces, bins):
    row_count, samples = flat_traces.shape
    bin_count = bins.shape[0]
    spectra = lax.dot_general(
        dft_table(samples, bins),
        flat_traces,
        (((1,), (1,)), ((), ())),
        precision=lax.Precision.HIGH,
        preferred_element_type=jnp.float32,
    )
    real_band = spectra[:bin_count].reshape(bin_count // SUB, SUB, row_count)
    imag_band = spectra[bin_count:].reshape(bin_count // SUB, SUB, row_count)
    band_power = jnp.mean(real_band * real_band + imag_band * imag_band, axis=1, keepdims=True)
    factor = lax.rsqrt(band_power + whiten_eps)
    stacked = jnp.stack([real_band * factor, imag_band * factor], axis=0)
    return stacked.reshape(2, bin_count, row_count).astype(jnp.bfloat16)


def slot_blocks(pair_list, pair_owner, slot_ids, per_slot):
    slot_match = (pair_owner[:, None] == slot_ids[None, :]).astype(jnp.int32)
    slot_rank = jnp.cumsum(slot_match, axis=0) - 1
    rank_ids = jnp.arange(per_slot, dtype=jnp.int32)
    selected = slot_match[:, :, None] * (slot_rank[:, :, None] == rank_ids[None, None, :]).astype(
        jnp.int32
    )
    first = jnp.sum(selected * pair_list[:, 0][:, None, None], axis=0)
    second = jnp.sum(selected * pair_list[:, 1][:, None, None], axis=0)
    return (first, second)


def shards(traces, pair_list, pair_owner):
    win_local, chan_local, samples = traces.shape
    bin_count = samples // 2
    bands = lax.axis_size("band")
    owners = lax.axis_size("pair")
    band_bins = bin_count // bands
    per_device = chan_local // BLOCK
    per_slot = pair_list.shape[0] // (owners * SLOTS)
    flat = traces.reshape(win_local * chan_local, samples)
    halves = 2
    half_bins = band_bins // halves
    edges = [0, band_bins // 2, 3 * band_bins // 4, band_bins]
    spans = []
    for half in range(halves):
        ids = np.arange(bands * half_bins)
        bins = ids // half_bins * band_bins + half * half_bins + ids % half_bins
        whitened = whiten(flat, bins)
        whitened = whitened.reshape(2, bands, half_bins, win_local, per_device, BLOCK)
        spans.append(jnp.transpose(whitened, (1, 4, 0, 3, 2, 5)))
    pieces = []
    for low, high in zip(edges[:-1], edges[1:]):
        parts = []
        for half in range(halves):
            start = max(low, half * half_bins)
            stop = min(high, (half + 1) * half_bins)
            if start < stop:
                parts.append(
                    spans[half][:, :, :, :, start - half * half_bins : stop - half * half_bins, :]
                )
        chunk_bins = parts[0] if len(parts) == 1 else jnp.concatenate(parts, axis=4)
        pieces.append(lax.all_to_all(chunk_bins, "band", split_axis=0, concat_axis=0, tiled=True))
    chunks = len(pieces)
    device_index = lax.axis_index("pair")
    slot_ids = device_index * SLOTS + jnp.arange(SLOTS, dtype=jnp.int32)
    first, second = slot_blocks(pair_list, pair_owner, slot_ids, per_slot)
    wanted = jnp.concatenate([first.reshape(-1), second.reshape(-1)])
    picks = (wanted[:, None] == jnp.arange(owners * per_device, dtype=jnp.int32)[None, :]).astype(
        jnp.bfloat16
    )
    products = []
    for part in range(chunks):
        piece = jnp.transpose(pieces[part], (1, 0, 2, 3, 4, 5))
        gathered = lax.all_gather(piece, "pair", axis=0, tiled=True)
        if part == chunks - 1 and part >= 1:
            gathered, products[-1] = lax.optimization_barrier((gathered, products[-1]))
        rows = gathered.shape[0]
        chosen = jnp.dot(picks, gathered.reshape(rows, -1), preferred_element_type=jnp.bfloat16)
        chosen = chosen.reshape(2, SLOTS, per_slot, *gathered.shape[1:])
        left = chosen[0]
        right = chosen[1]
        rotated = jnp.stack([-right[:, :, :, 1], right[:, :, :, 0]], axis=3)
        paired = jnp.stack([right, rotated], axis=1)
        product = jnp.einsum(
            "stgkwfa,sptgkwfb->spabf", left, paired, preferred_element_type=jnp.float32
        )
        product = product.astype(jnp.bfloat16)
        if part + 2 < chunks:
            pieces[part + 2], product = lax.optimization_barrier((pieces[part + 2], product))
        products.append(product)
    out = jnp.zeros((SLOTS, 2, BLOCK, BLOCK, band_bins), jnp.bfloat16)
    for part in range(chunks):
        out = lax.dynamic_update_slice_in_dim(out, products[part], edges[part], axis=4)
    return out


def solution(mesh):
    placed = (P("band", "pair", None), P(), P())
    return jax.shard_map(
        shards,
        mesh=mesh,
        in_specs=placed,
        out_specs=P("pair", None, None, None, "band"),
        check_vma=False,
    )
```

profile of v0, /device:TPU:1, one launch (start us, length us, event | category | flops | bytes accessed | tf_op | source)
XLA Modules:
  0.0 361.0 jit_solution(15198788224465309761)
XLA Ops:
  6.5 6.3 %fusion.52 = f32[512,1024]{1,0:T(8,128)S(1)} fusion(f32[512,1024]{1,0:T(8,128)} %constant.33.clone, f32[1024,1024]{1,0:T(8,128)} %bitcast.142), kind=kOutput, calls=%fused_computation.85 | convolution fusion | flops 3221225472 | bytes 8388608 | tf_op jit(solution)/shard_map/dot_general | solution.py:23
  14.5 19.0 %all_to_all.15 = bf16[4,2,2,4,64,128]{5,4,3,2,1,0:T(8,128)(2,1)S(1)} all-to-all(bf16[4,2,2,4,64,128]{5,4,3,2,1,0:T(8,128)(2,1)S(1)} %maximum_bitcast_fusion.4), channel_id=1, replica_groups=mesh['band'=4,'pair'=32] {'band'}, dimensions={0} | all-to-all | bytes 2097152 | tf_op jit(solution)/shard_map/all_to_all | solution.py:80
  34.7 5.7 %fusion.51 = f32[512,1024]{1,0:T(8,128)S(1)} fusion(f32[512,1024]{1,0:T(8,128)S(1)} %copy-done.1, f32[1024,1024]{1,0:T(8,128)} %bitcast.143), kind=kOutput, calls=%fused_computation.84 | convolution fusion | flops 3221225472 | bytes 8388608 | tf_op jit(solution)/shard_map/dot_general | solution.py:23
  42.9 10.1 %all_to_all.16 = bf16[4,2,2,4,32,128]{5,4,3,2,1,0:T(8,128)(2,1)S(1)} all-to-all(bf16[4,2,2,4,32,128]{5,4,3,2,1,0:T(8,128)(2,1)S(1)} %get-tuple-element.31), channel_id=1, replica_groups=mesh['band'=4,'pair'=32] {'band'}, dimensions={0} | all-to-all | bytes 1048576 | tf_op jit(solution)/shard_map/all_to_all | solution.py:80
  54.0 3.5 all-to-all-start
  59.5 91.2 %all-gather.4.cloned.1.call-done = bf16[64,4,2,4,64,128]{5,4,3,2,1,0:T(8,128)(2,1)} async-done(((bf16[2,4,2,4,64,128]{5,4,3,2,1,0:T(8,128)(2,1)}), bf16[64,4,2,4,64,128]{5,4,3,2,1,0:T(8,128)(2,1)}) %all-gather.4.cloned.1.call-update) | async-done | bytes 33554448 | tf_op jit(solution)/shard_map/all_gather | solution.py:92
  150.7 26.2 %fusion = bf16[16,262144]{1,0:T(8,128)(2,1)S(1)} fusion(bf16[8,8,2048,128]{3,2,1,0:T(8,128)(2,1)} %bitcast.133, s32[16]{0:T(128)S(1)} %pad_add_fusion), kind=kOutput, calls=%fused_computation | convolution fusion | flops 536871936 | bytes 41943104 | tf_op jit(solution)/shard_map/dot_general | solution.py:96
  176.8 1.2 slice_bitcast_fusion
  179.1 3.2 copy.66
  183.4 1.6 copy.92
  185.1 2.1 copy_negate_fusion
  187.2 2.9 maximum_bitcast_fusion
  190.1 17.0 %fusion.9 = bf16[2,2,128,128,64]{2,3,1,4,0:T(8,128)(2,1)} fusion(bf16[2,1,4,4,2,4,64,128]{7,5,2,4,3,1,6,0:T(4,128)(2,1)S(1)} %maximum_bitcast_fusion, bf16[2,1,4,4,2,4,64,128]{7,5,2,4,3,1,6,0:T(4,128)(2,1)S(1)} %copy.66, bf16[2,4,4,2,4,64,128,1]{6,5,4,3,2,1,0,7:T(8,128)(2,1)S(1)} %bitcast.144), kind=kOutput, calls=%fused_computation.10 | convolution fusion | flops 1094713344 | bytes 20971520 | tf_op jit(solution)/shard_map/stgkwfa,sptgkwfb->spabf/dot_general | solution.py:102
  208.0 16.9 %all-gather.8.cloned.1.call-done = bf16[64,4,2,4,32,128]{5,4,3,2,1,0:T(8,128)(2,1)} async-done(((bf16[2,4,2,4,32,128]{5,4,3,2,1,0:T(8,128)(2,1)}), bf16[64,4,2,4,32,128]{5,4,3,2,1,0:T(8,128)(2,1)}) %all-gather.8.cloned.1.call-update) | async-done | bytes 16777232 | tf_op jit(solution)/shard_map/all_gather | solution.py:92
  224.9 14.9 %fusion.6 = bf16[16,131072]{1,0:T(8,128)(2,1)S(1)} fusion(bf16[8,8,1024,128]{3,2,1,0:T(8,128)(2,1)} %bitcast.140, s32[16]{0:T(128)S(1)} %pad_add_fusion), kind=kOutput, calls=%fused_computation.6 | convolution fusion | flops 268436480 | bytes 20971584 | tf_op jit(solution)/shard_map/dot_general | solution.py:96
  243.8 1.4 maximum_bitcast_fusion.1
  245.1 6.3 %fusion.16 = bf16[2,2,128,128,32]{2,3,1,4,0:T(8,128)(2,1)} fusion(bf16[2,1,4,4,2,4,32,128]{7,5,2,4,3,1,6,0:T(4,128)(2,1)S(1)} %maximum_bitcast_fusion.1, bf16[2,1,4,4,2,4,32,128]{7,5,2,4,3,1,6,0:T(4,128)(2,1)S(1)} %copy.72, bf16[2,4,4,2,4,32,128,1]{6,5,4,3,2,1,0,7:T(8,128)(2,1)S(1)} %bitcast.147), kind=kOutput, calls=%fused_computation.17 | convolution fusion | flops 547356672 | bytes 10485760 | tf_op jit(solution)/shard_map/stgkwfa,sptgkwfb->spabf/dot_general | solution.py:102
  251.4 10.0 %dynamic_update_slice.9 = bf16[2,2,128,128,128]{2,3,1,4,0:T(8,128)(2,1)} pad(bf16[2,2,128,128,64]{2,3,1,4,0:T(8,128)(2,1)} %fusion.9, bf16[]{:T(256)} %constant.30.clone.1), padding=0_0x0_0x0_0x0_0x0_64 | pad | bytes 25165826 | tf_op jit(solution)/shard_map/dynamic_update_slice | solution.py:111
  261.4 37.8 %all-gather.6.cloned.1.call-done = bf16[64,4,2,4,32,128]{5,4,3,2,1,0:T(8,128)(2,1)} async-done(((bf16[2,4,2,4,32,128]{5,4,3,2,1,0:T(8,128)(2,1)}), bf16[64,4,2,4,32,128]{5,4,3,2,1,0:T(8,128)(2,1)}) %all-gather.6.cloned.1.call-update) | async-done | bytes 16777232 | tf_op jit(solution)/shard_map/all_gather | solution.py:92
  299.3 14.9 %fusion.3 = bf16[16,131072]{1,0:T(8,128)(2,1)S(1)} fusion(bf16[8,8,1024,128]{3,2,1,0:T(8,128)(2,1)} %bitcast.141, s32[16]{0:T(128)S(1)} %pad_add_fusion), kind=kOutput, calls=%fused_computation.3 | convolution fusion | flops 268436480 | bytes 20971584 | tf_op jit(solution)/shard_map/dot_general | solution.py:96
  318.1 1.4 maximum_bitcast_fusion.2
  319.5 2.8 constant_dynamic-update-slice_fusion
  322.3 6.2 %fusion.18 = bf16[2,2,128,128,128]{2,3,1,4,0:T(8,128)(2,1)} fusion(bf16[2,2,128,128,128]{2,3,1,4,0:T(8,128)(2,1)} %constant_dynamic-update-slice_fusion, bf16[2,1,4,4,2,4,32,128]{7,5,2,4,3,1,6,0:T(4,128)(2,1)S(1)} %maximum_bitcast_fusion.2, bf16[2,1,4,4,2,4,32,128]{7,5,2,4,3,1,6,0:T(4,128)(2,1)S(1)} %copy.76, ...), kind=kOutput, calls=%fused_computation.19 | convolution fusion | flops 547356672 | bytes 10485760 | tf_op jit(solution)/shard_map/stgkwfa,sptgkwfb->spabf/dot_general | solution.py:102
  328.5 25.8 %copy.78 = bf16[2,2,128,128,128]{4,3,2,1,0:T(8,128)(2,1)} copy(bf16[2,2,128,128,128]{2,3,1,4,0:T(8,128)(2,1)} %fusion.18) | data formatting | bytes 33554432 | tf_op jit(solution)/shard_map/dynamic_update_slice | solution.py:111
  (65 shorter events, 18.9 us)
Async XLA Ops:
  6.5 144.1 %all-gather.4.cloned.1.call-start = ((), (), s32[]{:S(2)}) async-start(), calls=%async_computation.3 | async-start | bytes 34603008 | tf_op jit(solution)/shard_map/all_gather | solution.py:92
  14.5 20.1 %copy-start.1 = (f32[512,1024]{1,0:T(8,128)S(1)}, f32[512,1024]{1,0:T(8,128)}, u32[]{:S(2)}) copy-start(f32[512,1024]{1,0:T(8,128)} %constant.34.clone) | copy-start | bytes 6291460
  34.6 190.3 %all-gather.8.cloned.1.call-start = ((), (), s32[]{:S(2)}) async-start(), calls=%async_computation.5 | async-start | bytes 17301504 | tf_op jit(solution)/shard_map/all_gather | solution.py:92
  41.9 15.9 %copy-start.2 = (s32[256]{0:T(256)S(1)}, s32[256]{0:T(256)}, u32[]{:S(2)}) copy-start(s32[256]{0:T(256)} %param.7) | copy-start | bytes 3076
  41.9 17.2 %copy-start.3 = (s32[256,2]{0,1:T(2,128)S(1)}, s32[256,2]{0,1:T(2,128)}, u32[]{:S(2)}) copy-start(s32[256,2]{0,1:T(2,128)} %param.6) | copy-start | bytes 6148
  54.0 153.2 %all-to-all-start = ((bf16[4,2,2,4,32,128]{5,4,3,2,1,0:T(8,128)(2,1)}), bf16[4,2,2,4,32,128]{5,4,3,2,1,0:T(8,128)(2,1)S(1)}, u32[]{:S(2)}, u32[]{:S(2)}) async-start(bf16[4,2,2,4,32,128]{5,4,3,2,1,0:T(8,128)(2,1)} %get-tuple-element.32), calls=%async_computation | async-start | bytes 1048576 | tf_op jit(solution)/shard_map/all_to_all | solution.py:80
  57.4 241.8 %all-gather.6.cloned.1.call-start = ((), (), s32[]{:S(2)}) async-start(), calls=%async_computation.4 | async-start | bytes 17301504 | tf_op jit(solution)/shard_map/all_gather | solution.py:92
  316.8 2.7 copy-start
Sparse Core Ops, SparseCore 0:
  34.7 115.8 all-gather.3
  152.9 71.9 all-gather.7
  227.1 72.0 all-gather.5
where the time goes:
time: 368 us; the launch traced here: 361 us
  waiting for transfers between devices  146 us (40%)
  matrix products  97.5 us (26%)
  local copies, waits for them, and re-layouts  59.3 us (16%)
  blocking collectives  29.1 us (8%)
  between operations  13.7 us (4%)
  other arithmetic  11.6 us (3%)
  starting transfers between devices  3.87 us (1%)
    all_gather x3, waiting for transfers between devices, shards(): gathered = lax.all_gather(piece, 'pair', axis=0, tiled=True)  146 us
    dot_general x3, matrix products, shards(): jnp.dot(picks, gathered.reshape(rows, -1), preferred_element_type=jnp.bfl...  56 us
    dynamic_update_slice x3, local copies, waits for them, and re-layouts, shards(): lax.dynamic_update_slice_in_dim(out, products[part], edges[part], axis=4)  38.7 us
    dot_general x3, matrix products, shards(): jnp.einsum('stgkwfa,sptgkwfb->spabf', left, paired, preferred_element_typ...  29.5 us
    all_to_all x2, blocking collectives, shards(): lax.all_to_all(chunk_bins, 'band', split_axis=0, concat_axis=0, tiled=True)  29.1 us
    dot_general x2, matrix products, whiten(): lax.dot_general(dft_table(samples, bins), flat_traces, (((1,), (1,)), (()...  12 us
  transfers between devices with their start and end apart: 4, of which 3 were waited for; matrix products, arithmetic and copies ran while one was open for 29% of the time, Pallas kernels for 0%

commit v1 on v0

--- a/solution.py
+++ b/solution.py
@@ -89,7 +89,9 @@
     products = []
     for part in range(chunks):
         piece = jnp.transpose(pieces[part], (1, 0, 2, 3, 4, 5))
-        gathered = lax.all_gather(piece, "pair", axis=0, tiled=True)
+        gathered = jnp.concatenate(
+            lax.all_to_all(jnp.stack([piece] * lax.axis_size("pair")), "pair", 0, 0), axis=0
+        )
         if part == chunks - 1 and part >= 1:
             gathered, products[-1] = lax.optimization_barrier((gathered, products[-1]))
         rows = gathered.shape[0]

time: 368 us -> 1030 us (2.80); the launches traced: 361 us -> 1010 us
  waiting for transfers between devices: 146 us -> 685 us
  local copies, waits for them, and re-layouts: 59.3 us -> 131 us
  starting transfers between devices: 3.87 us -> 65.1 us
  other arithmetic: 11.6 us -> 27.2 us
  matrix products: 97.5 us -> 82.1 us
  between operations: 13.7 us -> 0.84 us
  blocking collectives: 29.1 us -> 17.5 us
    all_to_all x0 -> x3, waiting for transfers between devices: none -> 679 us  [shards(): lax.all_to_all(jnp.stack([piece] * lax.axis_size('pair')), 'pair', 0, 0)]
    all_gather x3 -> x0, waiting for transfers between devices: 146 us -> none  [shards(): gathered = lax.all_gather(piece, 'pair', axis=0, tiled=True)]
    another operation x0 -> x5, local copies, waits for them, and re-layouts: none -> 68.7 us  [the longest x2 44.9 us: shards(): gathered.reshape(rows, -1)]
    all_to_all x0 -> x3, starting transfers between devices: none -> 56.8 us  [shards(): lax.all_to_all(jnp.stack([piece] * lax.axis_size('pair')), 'pair', 0, 0)]
    dot_general x3, matrix products: 56 us -> 39.4 us  [shards(): jnp.dot(picks, gathered.reshape(rows, -1), preferred_element_type=jnp.bfl...]
    another operation x3, other arithmetic: 5.58 us -> 18.6 us  [shards(): paired = jnp.stack([right, rotated], axis=1)]
    all_to_all x2 -> x1, blocking collectives: 29.1 us -> 17.5 us  [shards(): lax.all_to_all(chunk_bins, 'band', split_axis=0, concat_axis=0, tiled=True)]
  transfers between devices with their start and end apart: 4 -> 5, of which waited for: 3 -> 4; matrix products, arithmetic and copies ran while one was open for 29% -> 15% of each run, Pallas kernels for 0% -> 0%
where the time goes in v1:
time: 1030 us; the launch traced here: 1010 us
  waiting for transfers between devices  685 us (67%)
  local copies, waits for them, and re-layouts  131 us (13%)
  matrix products  82.1 us (8%)
  starting transfers between devices  65.1 us (6%)
  other arithmetic  27.2 us (3%)
  blocking collectives  17.5 us (2%)
    all_to_all x3, waiting for transfers between devices, shards(): lax.all_to_all(jnp.stack([piece] * lax.axis_size('pair')), 'pair', 0, 0)  679 us
    all_to_all x3, starting transfers between devices, shards(): lax.all_to_all(jnp.stack([piece] * lax.axis_size('pair')), 'pair', 0, 0)  56.8 us
    another operation x2, local copies, waits for them, and re-layouts, shards(): gathered.reshape(rows, -1)  44.9 us
    dot_general x3, matrix products, shards(): jnp.dot(picks, gathered.reshape(rows, -1), preferred_element_type=jnp.bfl...  39.4 us
    dynamic_update_slice x3, local copies, waits for them, and re-layouts, shards(): lax.dynamic_update_slice_in_dim(out, products[part], edges[part], axis=4)  38.9 us
    dot_general x3, matrix products, shards(): jnp.einsum('stgkwfa,sptgkwfb->spabf', left, paired, preferred_element_typ...  30.7 us
    another operation x3, local copies, waits for them, and re-layouts, shards(): jnp.stack([piece] * lax.axis_size('pair'))  23.8 us
  transfers between devices with their start and end apart: 5, of which 4 were waited for; matrix products, arithmetic and copies ran while one was open for 15% of the time, Pallas kernels for 0%

profile of v1, /device:TPU:1, one launch (start us, length us, event | category | flops | bytes accessed | tf_op | source)
XLA Modules:
  0.0 1008.8 jit_solution(11864985722350135504)
XLA Ops:
  0.0 6.3 fusion.47
  15.8 5.7 fusion.48
  24.3 17.5 %all_to_all.30 = bf16[4,2,2,4,64,128]{5,1,3,4,2,0:T(2,128)(2,1)S(1)} all-to-all(bf16[4,2,2,4,64,128]{5,1,3,4,2,0:T(2,128)(2,1)S(1)} %maximum_bitcast_fusion.4), channel_id=1, replica_groups=mesh['band'=4,'pair'=32] {'band'}, dimensions={0} | all-to-all | bytes 2097152 | tf_op jit(solution)/shard_map/all_to_all | solution.py:80
  45.5 6.6 all-to-all-done.4
  52.1 11.2 %stack.42 = bf16[32,2,4,2,4,64,128]{6,5,4,3,2,1,0:T(8,128)(2,1)} broadcast(bf16[2,4,2,4,64,128]{5,4,3,2,1,0:T(8,128)(2,1)S(1)} %copy.65), dimensions={1,2,3,4,5,6} | broadcast | bytes 34603008 | tf_op jit(solution)/shard_map/stack | solution.py:93
  63.4 12.5 %all-to-all-start.2 = ((bf16[32,2,4,2,4,64,128]{6,5,4,3,2,1,0:T(8,128)(2,1)}), bf16[32,2,4,2,4,64,128]{6,5,4,3,2,1,0:T(8,128)(2,1)}, u32[]{:S(2)}, u32[]{:S(2)}) async-start(bf16[32,2,4,2,4,64,128]{6,5,4,3,2,1,0:T(8,128)(2,1)} %stack.42), calls=%async_computation.2 | async-start | bytes 67108864 | tf_op jit(solution)/shard_map/all_to_all | solution.py:93
  76.0 416.6 %all-to-all-done.2 = bf16[32,2,4,2,4,64,128]{6,5,4,3,2,1,0:T(8,128)(2,1)} async-done(((bf16[32,2,4,2,4,64,128]{6,5,4,3,2,1,0:T(8,128)(2,1)}), bf16[32,2,4,2,4,64,128]{6,5,4,3,2,1,0:T(8,128)(2,1)}, u32[]{:S(2)}, u32[]{:S(2)}) %all-to-all-start.2) | async-done | bytes 33554464 | tf_op jit(solution)/shard_map/all_to_all | solution.py:93
  492.6 6.4 stack.47
  498.9 27.5 %all-to-all-start.5 = ((bf16[32,2,4,2,4,32,128]{6,5,4,3,2,1,0:T(8,128)(2,1)}), bf16[32,2,4,2,4,32,128]{6,5,4,3,2,1,0:T(8,128)(2,1)}, u32[]{:S(2)}, u32[]{:S(2)}) async-start(bf16[32,2,4,2,4,32,128]{6,5,4,3,2,1,0:T(8,128)(2,1)} %stack.47), calls=%async_computation.5 | async-start | bytes 33554432 | tf_op jit(solution)/shard_map/all_to_all | solution.py:93
  528.1 28.2 %reshape_reshape.6 = bf16[64,262144]{1,0:T(8,128)(2,1)} reshape(bf16[32,2,4,2,4,64,128]{6,5,4,3,2,1,0:T(8,128)(2,1)} %all-to-all-done.2) | data formatting | bytes 67108864 | tf_op jit(solution)/shard_map/reshape;reshape | solution.py:98
  556.3 16.4 %fusion.35 = bf16[16,262144]{1,0:T(8,128)(2,1)} fusion(bf16[64,262144]{1,0:T(8,128)(2,1)} %reshape_reshape.6, s32[16]{0:T(128)S(1)} %pad_add_fusion), kind=kOutput, calls=%fused_computation.59 | convolution fusion | flops 536871936 | bytes 41943104 | tf_op jit(solution)/shard_map/dot_general | solution.py:98
  586.0 15.9 %maximum_bitcast_fusion = bf16[2,1,4,4,2,4,64,128]{7,5,2,4,3,1,6,0:T(4,128)(2,1)} fusion(bf16[2,4,4,1,4,64,128]{6,4,1,3,2,5,0:T(4,128)(2,1)S(1)} %copy.94, bf16[2,4,4,1,4,64,128]{6,4,1,3,2,5,0:T(4,128)(2,1)S(1)} %copy_negate_fusion), kind=kLoop, calls=%fused_computation.16 | loop fusion | flops 2097152 | bytes 8388608 | tf_op jit(solution)/shard_map/stack | solution.py:103
  601.9 18.3 %fusion.3 = bf16[2,2,128,128,64]{2,3,1,4,0:T(8,128)(2,1)} fusion(bf16[2,1,4,4,2,4,64,128]{7,5,2,4,3,1,6,0:T(4,128)(2,1)} %maximum_bitcast_fusion, bf16[2,1,4,4,2,4,64,128]{7,5,2,4,3,1,6,0:T(4,128)(2,1)S(1)} %copy.68, bf16[2,4,4,2,4,64,128,1]{6,5,4,3,2,1,0,7:T(8,128)(2,1)S(1)} %bitcast.142), kind=kOutput, calls=%fused_computation.4 | convolution fusion | flops 1094713344 | bytes 20971520 | tf_op jit(solution)/shard_map/stgkwfa,sptgkwfb->spabf/dot_general | solution.py:104
  621.3 106.7 %all-to-all-done.5 = bf16[32,2,4,2,4,32,128]{6,5,4,3,2,1,0:T(8,128)(2,1)} async-done(((bf16[32,2,4,2,4,32,128]{6,5,4,3,2,1,0:T(8,128)(2,1)}), bf16[32,2,4,2,4,32,128]{6,5,4,3,2,1,0:T(8,128)(2,1)}, u32[]{:S(2)}, u32[]{:S(2)}) %all-to-all-start.5) | async-done | bytes 16777248 | tf_op jit(solution)/shard_map/all_to_all | solution.py:93
  728.0 6.2 stack.46
  734.2 16.9 %all-to-all-start.3 = ((bf16[32,2,4,2,4,32,128]{6,5,4,3,2,1,0:T(8,128)(2,1)}), bf16[32,2,4,2,4,32,128]{6,5,4,3,2,1,0:T(8,128)(2,1)}, u32[]{:S(2)}, u32[]{:S(2)}) async-start(bf16[32,2,4,2,4,32,128]{6,5,4,3,2,1,0:T(8,128)(2,1)} %stack.46), calls=%async_computation.3 | async-start | bytes 33554432 | tf_op jit(solution)/shard_map/all_to_all | solution.py:93
  751.1 16.7 %reshape_reshape.7 = bf16[64,131072]{1,0:T(8,128)(2,1)} reshape(bf16[32,2,4,2,4,32,128]{6,5,4,3,2,1,0:T(8,128)(2,1)} %all-to-all-done.5) | data formatting | bytes 33554432 | tf_op jit(solution)/shard_map/reshape;reshape | solution.py:98
  767.7 8.1 fusion.34
  780.8 6.2 fusion.10
  787.1 10.2 %dynamic_update_slice.9 = bf16[2,2,128,128,128]{2,3,1,4,0:T(8,128)(2,1)} pad(bf16[2,2,128,128,64]{2,3,1,4,0:T(8,128)(2,1)} %fusion.3, bf16[]{:T(256)} %constant.30.clone.1), padding=0_0x0_0x0_0x0_0x0_64 | pad | bytes 25165826 | tf_op jit(solution)/shard_map/dynamic_update_slice | solution.py:113
  797.3 155.4 %all-to-all-done.3 = bf16[32,2,4,2,4,32,128]{6,5,4,3,2,1,0:T(8,128)(2,1)} async-done(((bf16[32,2,4,2,4,32,128]{6,5,4,3,2,1,0:T(8,128)(2,1)}), bf16[32,2,4,2,4,32,128]{6,5,4,3,2,1,0:T(8,128)(2,1)}, u32[]{:S(2)}, u32[]{:S(2)}) %all-to-all-start.3) | async-done | bytes 16777248 | tf_op jit(solution)/shard_map/all_to_all | solution.py:93
  952.7 14.9 %fusion = bf16[16,131072]{1,0:T(8,128)(2,1)S(1)} fusion(bf16[8,8,1024,128]{3,2,1,0:T(8,128)(2,1)} %bitcast.62, s32[16]{0:T(128)S(1)} %pad_add_fusion), kind=kOutput, calls=%fused_computation | convolution fusion | flops 268436480 | bytes 20971584 | tf_op jit(solution)/shard_map/dot_general | solution.py:98
  976.3 6.2 fusion.12
  982.5 25.8 %copy.80 = bf16[2,2,128,128,128]{4,3,2,1,0:T(8,128)(2,1)} copy(bf16[2,2,128,128,128]{2,3,1,4,0:T(8,128)(2,1)} %fusion.12) | data formatting | bytes 33554432 | tf_op jit(solution)/shard_map/dynamic_update_slice | solution.py:113
  (64 shorter events, 45.7 us)
Async XLA Ops:
  9.1 6.8 copy-start.1
  11.0 13.3 %all-to-all-start = ((bf16[4,2,2,4,32,128]{5,1,3,4,2,0:T(2,128)(2,1)}), bf16[4,2,2,4,32,128]{5,1,3,4,2,0:T(2,128)(2,1)}, u32[]{:S(2)}, u32[]{:S(2)}) async-start(bf16[4,2,2,4,32,128]{5,1,3,4,2,0:T(2,128)(2,1)} %get-tuple-element.32), calls=%async_computation | async-start | bytes 1048576 | tf_op jit(solution)/shard_map/all_to_all | solution.py:80
  41.8 10.4 %all-to-all-start.4 = ((bf16[4,2,2,4,32,128]{5,1,3,4,2,0:T(2,128)(2,1)}), bf16[4,2,2,4,32,128]{5,1,3,4,2,0:T(2,128)(2,1)S(1)}, u32[]{:S(2)}, u32[]{:S(2)}) async-start(bf16[4,2,2,4,32,128]{5,1,3,4,2,0:T(2,128)(2,1)} %get-tuple-element.31), calls=%async_computation.4 | async-start | bytes 1048576 | tf_op jit(solution)/shard_map/all_to_all | solution.py:80
  63.4 429.2 %all-to-all-start.2 = ((bf16[32,2,4,2,4,64,128]{6,5,4,3,2,1,0:T(8,128)(2,1)}), bf16[32,2,4,2,4,64,128]{6,5,4,3,2,1,0:T(8,128)(2,1)}, u32[]{:S(2)}, u32[]{:S(2)}) async-start(bf16[32,2,4,2,4,64,128]{6,5,4,3,2,1,0:T(8,128)(2,1)} %stack.42), calls=%async_computation.2 | async-start | bytes 67108864 | tf_op jit(solution)/shard_map/all_to_all | solution.py:93
  498.9 27.5 %copy-start.2 = (s32[256]{0:T(256)S(1)}, s32[256]{0:T(256)}, u32[]{:S(2)}) copy-start(s32[256]{0:T(256)} %param.7) | copy-start | bytes 3076
  498.9 28.7 %copy-start.3 = (s32[256,2]{0,1:T(2,128)S(1)}, s32[256,2]{0,1:T(2,128)}, u32[]{:S(2)}) copy-start(s32[256,2]{0,1:T(2,128)} %param.6) | copy-start | bytes 6148
  498.9 229.0 %all-to-all-start.5 = ((bf16[32,2,4,2,4,32,128]{6,5,4,3,2,1,0:T(8,128)(2,1)}), bf16[32,2,4,2,4,32,128]{6,5,4,3,2,1,0:T(8,128)(2,1)}, u32[]{:S(2)}, u32[]{:S(2)}) async-start(bf16[32,2,4,2,4,32,128]{6,5,4,3,2,1,0:T(8,128)(2,1)} %stack.47), calls=%async_computation.5 | async-start | bytes 33554432 | tf_op jit(solution)/shard_map/all_to_all | solution.py:93
  734.2 218.5 %all-to-all-start.3 = ((bf16[32,2,4,2,4,32,128]{6,5,4,3,2,1,0:T(8,128)(2,1)}), bf16[32,2,4,2,4,32,128]{6,5,4,3,2,1,0:T(8,128)(2,1)}, u32[]{:S(2)}, u32[]{:S(2)}) async-start(bf16[32,2,4,2,4,32,128]{6,5,4,3,2,1,0:T(8,128)(2,1)} %stack.46), calls=%async_computation.3 | async-start | bytes 33554432 | tf_op jit(solution)/shard_map/all_to_all | solution.py:93
  971.3 2.2 copy-start
